TPU v7x, 32 devices: a whole 2x2x4 slice. The times are simulated.
32 devices in a mesh: slab: 2 (over y), genome: 4 (over x, core), group: 4 (over z).
Axes of the slice: x: 2, y: 2, z: 4, core: 2. Of those that a mesh axis runs over, the one named last changes fastest.
Arguments:
- genotypes: bfloat16 [640, 12288], P(None, ('slab', 'genome', 'group')), parts along dimension 1, may hold values from -6 to 6
Outputs:
- ld_score: float32 [12288], P(('slab', 'genome', 'group')), parts along dimension 0
There are 2 independent parts, one for each index of `slab`. A program takes and returns all parts, laid end to end along the dimension named above; each array names one. Nothing has to cross between parts.
All inputs are finite; a program needn't handle non-finite values.
Results may differ from a plain program's by a relative error of at most 0.0003.
Values may be sent and summed in bfloat16 or wider, within the bound.
No kernel may reach another device: no remote copies, remote signals or barrier semaphores. Data moves between devices by JAX's collectives and lax.ppermute only.
A program may use at most 64 MiB of HBM per device.

v0:
```python
import jax
import jax.numpy as jnp
from jax import lax
from jax.sharding import PartitionSpec as P


def passed_along(block, axis, distance):
    devices = range(lax.axis_size(axis))
    route = [(i - distance, i) for i in devices if i - distance in devices]
    return lax.ppermute(block, axis, route)


def per_device(genotypes):
    scaling = 1.0 / genotypes.shape[0]

    def squares(columns):
        band = (
            lax.dot_general(
                genotypes, columns, (((0,), (0,)), ((), ())), preferred_element_type=jnp.float32
            )
            * scaling
        )
        return jnp.sum(band * band, axis=1)

    gathered = lax.all_gather(genotypes, "group", axis=1, tiled=True)
    following = passed_along(gathered, "genome", -1)
    ld_score = squares(gathered) + squares(following)
    return ld_score


def solution(mesh):
    placed = (P(None, ("slab", "genome", "group")),)
    return jax.shard_map(
        per_device,
        mesh=mesh,
        in_specs=placed,
        out_specs=P(("slab", "genome", "group")),
        check_vma=False,
    )
```

profile of v0, /device:TPU:1, one launch (start us, length us, event | category | flops | bytes accessed | tf_op | source)
XLA Modules:
  0.0 89.7 jit_solution(2843091351955072725)
XLA Ops:
  6.5 0.0 all-gather.2.cloned.1.call-start
  6.5 0.0 copy-start
  6.5 0.7 all-gather.2.cloned.1.call-update
  7.3 47.5 %all-gather.2.cloned.1.call-done = bf16[640,1536]{1,0:T(8,128)(2,1)} async-done(((bf16[640,384]{1,0:T(8,128)(2,1)}), bf16[640,1536]{1,0:T(8,128)(2,1)}) %all-gather.2.cloned.1.call-update) | async-done | bytes 1966096 | tf_op jit(solution)/shard_map/all_gather | solution.py:25
  54.7 2.7 %collective-permute-start = (bf16[640,1536]{1,0:T(8,128)(2,1)}, bf16[640,1536]{1,0:T(8,128)(2,1)S(1)}, u32[]{:S(2)}, u32[]{:S(2)}) collective-permute-start(bf16[640,1536]{1,0:T(8,128)(2,1)} %all-gather.2.cloned.1.call-done), channel_id=1, source_target_pairs={{4,0},{8,4},{12,8},{5,1},{9,5},{13,9},{6,2},{10,6},{14,10},{7,3},{... | collective-permute-start | bytes 5898248 | tf_op jit(solution)/shard_map/ppermute | solution.py:10
  57.5 2.9 %fusion.2 = f32[384]{0:T(512)S(1)} fusion(bf16[640,384]{1,0:T(8,128)(2,1)} %param.1, bf16[640,1536]{1,0:T(8,128)(2,1)} %all-gather.2.cloned.1.call-done), kind=kOutput, calls=%fused_computation.4 | convolution fusion | flops 756743808 | bytes 2459136 | tf_op jit(solution)/shard_map/dot_general | solution.py:18
  60.4 20.7 %collective-permute-done = bf16[640,1536]{1,0:T(8,128)(2,1)S(1)} collective-permute-done((bf16[640,1536]{1,0:T(8,128)(2,1)}, bf16[640,1536]{1,0:T(8,128)(2,1)S(1)}, u32[]{:S(2)}, u32[]{:S(2)}) %collective-permute-start) | collective-permute-done | bytes 1966112 | tf_op jit(solution)/shard_map/ppermute | solution.py:10
  81.1 0.0 copy-done
  81.1 1.2 %fusion.3 = f32[384]{0:T(512)S(1)} fusion(bf16[640,384]{1,0:T(8,128)(2,1)S(1)} %copy-done, bf16[640,1536]{1,0:T(8,128)(2,1)S(1)} %collective-permute-done), kind=kOutput, calls=%fused_computation.5 | convolution fusion | flops 756743808 | bytes 2459136 | tf_op jit(solution)/shard_map/dot_general | solution.py:18
  82.2 0.6 add.3
Async XLA Ops:
  6.5 48.2 %all-gather.2.cloned.1.call-start = ((), (), s32[]{:S(2)}) async-start(), calls=%async_computation | async-start | bytes 2457600 | tf_op jit(solution)/shard_map/all_gather | solution.py:25
  6.5 74.5 %copy-start = (bf16[640,384]{1,0:T(8,128)(2,1)S(1)}, bf16[640,384]{1,0:T(8,128)(2,1)}, u32[]{:S(2)}) copy-start(bf16[640,384]{1,0:T(8,128)(2,1)} %param.1) | copy-start | bytes 1474564
  54.7 26.3 %collective-permute-start = (bf16[640,1536]{1,0:T(8,128)(2,1)}, bf16[640,1536]{1,0:T(8,128)(2,1)S(1)}, u32[]{:S(2)}, u32[]{:S(2)}) collective-permute-start(bf16[640,1536]{1,0:T(8,128)(2,1)} %all-gather.2.cloned.1.call-done), channel_id=1, source_target_pairs={{4,0},{8,4},{12,8},{5,1},{9,5},{13,9},{6,2},{10,6},{14,10},{7,3},{... | collective-permute-start | bytes 5898248 | tf_op jit(solution)/shard_map/ppermute | solution.py:10
Sparse Core Ops, SparseCore 0:
  9.0 45.7 all-gather.1
where the time goes:
time: 89.8 us; the launch traced here: 89.7 us
  waiting for transfers between devices  68.8 us (77%)
  between operations  13.4 us (15%)
  matrix products  4.09 us (5%)
  starting transfers between devices  2.75 us (3%)
    all_gather x1, waiting for transfers between devices, per_device(): gathered = lax.all_gather(genotypes, 'group', axis=1, tiled=True)  47.5 us
    ppermute x1, waiting for transfers between devices, passed_along(): return lax.ppermute(block, axis, route)  20.7 us
    dot_general x2, matrix products, squares(): lax.dot_general(genotypes, columns, (((0,), (0,)), ((), ())), preferred_e...  4.09 us
    ppermute x1, starting transfers between devices, passed_along(): return lax.ppermute(block, axis, route)  2.75 us
  transfers between devices with their start and end apart: 2, of which 2 were waited for; matrix products, arithmetic and copies ran while one was open for 3% of the time, Pallas kernels for 0%

commit v1 on v0

--- a/solution.py
+++ b/solution.py
@@ -22,7 +22,19 @@
         )
         return jnp.sum(band * band, axis=1)
 
-    gathered = lax.all_gather(genotypes, "group", axis=1, tiled=True)
+    many = lax.psum(1, "group")
+    bank = tuple(((pp, (pp + 1) % many) for pp in range(many)))
+    slots = tuple(((pp, (pp - 1) % many) for pp in range(many)))
+    piece_next, state_now = ([genotypes], [genotypes])
+    for _ in range(many // 2):
+        small = lax.ppermute(piece_next[-1], "group", perm=bank)
+        piece_next.append(small)
+    for _ in range((many - 1) // 2):
+        f_now = lax.ppermute(state_now[-1], "group", slots)
+        state_now.append(f_now)
+    current_value = jnp.concatenate([*piece_next[::-1], *state_now[1:]], axis=1)
+    k_now = lax.axis_index("group")
+    gathered = jnp.roll(current_value, (k_now - many // 2) * genotypes.shape[1], axis=1)
     following = passed_along(gathered, "genome", -1)
     ld_score = squares(gathered) + squares(following)
     return ld_score

time: 89.8 us -> 68.8 us (0.77)
  waiting for transfers between devices: 68.8 us -> 52.7 us
  between operations: 13.4 us -> 0.1 us
  starting transfers between devices: 2.75 us -> 9.44 us
  local copies, waits for them, and re-layouts: 0.01 us -> 3.06 us
  matrix products: 4.09 us -> 2.69 us
    all_gather x1 -> x0, waiting for transfers between devices: 47.5 us -> none  [per_device(): gathered = lax.all_gather(genotypes, 'group', axis=1, tiled=True)]
    ppermute x0 -> x3, waiting for transfers between devices: none -> 30.9 us  [the longest x2 23.4 us: per_device(): small = lax.ppermute(piece_next[-1], 'group', perm=bank)]
    ppermute x0 -> x3, starting transfers between devices: none -> 5.39 us  [the longest x1 3.26 us: per_device(): f_now = lax.ppermute(state_now[-1], 'group', slots)]
    unnamed x2 -> x9, local copies, waits for them, and re-layouts: 0.01 us -> 1.8 us
    dot_general x2, matrix products: 4.09 us -> 2.69 us  [squares(): lax.dot_general(genotypes, columns, (((0,), (0,)), ((), ())), preferred_e...]
    ppermute x1, starting transfers between devices: 2.75 us -> 4.05 us  [passed_along(): return lax.ppermute(block, axis, route)]
    ppermute x1, waiting for transfers between devices: 20.7 us -> 21.9 us  [passed_along(): return lax.ppermute(block, axis, route)]
    dynamic_slice x0 -> x1, local copies, waits for them, and re-layouts: none -> 1.14 us  [per_device(): jnp.roll(current_value, (k_now - many // 2) * genotypes.shape[1], axis=1)]
  transfers between devices with their start and end apart: 2 -> 4, of which waited for: 2 -> 4; matrix products, arithmetic and copies ran while one was open for 3% -> 4% of each run, Pallas kernels for 0% -> 0%
where the time goes in v1:
time: 68.8 us; the launch traced here: 68.6 us
  waiting for transfers between devices  52.7 us (77%)
  starting transfers between devices  9.44 us (14%)
  local copies, waits for them, and re-layouts  3.06 us (4%)
  matrix products  2.69 us (4%)
    ppermute x2, waiting for transfers between devices, per_device(): small = lax.ppermute(piece_next[-1], 'group', perm=bank)  23.4 us
    ppermute x1, waiting for transfers between devices, passed_along(): return lax.ppermute(block, axis, route)  21.9 us
    ppermute x1, waiting for transfers between devices, per_device(): f_now = lax.ppermute(state_now[-1], 'group', slots)  7.5 us
    ppermute x1, starting transfers between devices, passed_along(): return lax.ppermute(block, axis, route)  4.05 us
    ppermute x1, starting transfers between devices, per_device(): f_now = lax.ppermute(state_now[-1], 'group', slots)  3.26 us
    dot_general x2, matrix products, squares(): lax.dot_general(genotypes, columns, (((0,), (0,)), ((), ())), preferred_e...  2.69 us
    ppermute x2, starting transfers between devices, per_device(): small = lax.ppermute(piece_next[-1], 'group', perm=bank)  2.13 us
    unnamed x9, local copies, waits for them, and re-layouts  1.8 us
  transfers between devices with their start and end apart: 4, of which 4 were waited for; matrix products, arithmetic and copies ran while one was open for 4% of the time, Pallas kernels for 0%

profile of v1, /device:TPU:1, one launch (start us, length us, event | category | flops | bytes accessed | tf_op | source)
XLA Modules:
  0.0 68.6 jit_solution(15264377606346620041)
XLA Ops:
  0.0 0.0 copy-start
  0.0 2.1 %collective-permute-start = (bf16[640,384]{1,0:T(8,128)(2,1)}, bf16[640,384]{1,0:T(8,128)(2,1)S(1)}, u32[]{:S(2)}, u32[]{:S(2)}) collective-permute-start(bf16[640,384]{1,0:T(8,128)(2,1)} %param.1), channel_id=1, source_target_pairs={{0,1},{1,2},{2,3},{3,0},{4,5},{5,6},{6,7},{7,4},{8,9},{9,10},{10,1... | collective-permute-start | bytes 1474568 | tf_op jit(solution)/shard_map/ppermute | solution.py:30
  2.1 13.3 %collective-permute-done = bf16[640,384]{1,0:T(8,128)(2,1)S(1)} collective-permute-done((bf16[640,384]{1,0:T(8,128)(2,1)}, bf16[640,384]{1,0:T(8,128)(2,1)S(1)}, u32[]{:S(2)}, u32[]{:S(2)}) %collective-permute-start) | collective-permute-done | bytes 491552 | tf_op jit(solution)/shard_map/ppermute | solution.py:30
  15.4 0.0 collective-permute-start.1
  15.4 3.3 %collective-permute-start.2 = (bf16[640,384]{1,0:T(8,128)(2,1)}, bf16[640,384]{1,0:T(8,128)(2,1)S(1)}, u32[]{:S(2)}, u32[]{:S(2)}) collective-permute-start(bf16[640,384]{1,0:T(8,128)(2,1)} %param.1), channel_id=1, source_target_pairs={{0,3},{1,0},{2,1},{3,2},{4,7},{5,4},{6,5},{7,6},{8,11},{9,8},{10,9... | collective-permute-start | bytes 1474568 | tf_op jit(solution)/shard_map/ppermute | solution.py:33
  18.6 10.1 %collective-permute-done.1 = bf16[640,384]{1,0:T(8,128)(2,1)S(1)} collective-permute-done((bf16[640,384]{1,0:T(8,128)(2,1)S(1)}, bf16[640,384]{1,0:T(8,128)(2,1)S(1)}, u32[]{:S(2)}, u32[]{:S(2)}) %collective-permute-start.1) | collective-permute-done | bytes 491552 | tf_op jit(solution)/shard_map/ppermute | solution.py:30
  28.8 0.1 constant_dynamic-update-slice_fusion.7
  28.8 0.1 constant_dynamic-update-slice_fusion.6
  29.0 1.1 %constant_dynamic-update-slice_fusion.5 = bf16[640,3072]{1,0:T(8,128)(2,1)S(1)} fusion(bf16[640,3072]{1,0:T(8,128)(2,1)S(1)} %constant_dynamic-update-slice_fusion.6, bf16[640,384]{1,0:T(8,128)(2,1)} %param.1), kind=kLoop, calls=%fused_computation.11 | loop fusion | bytes 983040
  30.1 7.5 %collective-permute-done.2 = bf16[640,384]{1,0:T(8,128)(2,1)S(1)} collective-permute-done((bf16[640,384]{1,0:T(8,128)(2,1)}, bf16[640,384]{1,0:T(8,128)(2,1)S(1)}, u32[]{:S(2)}, u32[]{:S(2)}) %collective-permute-start.2) | collective-permute-done | bytes 491552 | tf_op jit(solution)/shard_map/ppermute | solution.py:33
  37.6 0.1 constant_dynamic-update-slice_fusion.4
  37.7 0.1 constant_dynamic-update-slice_fusion.3
  37.9 0.1 constant_dynamic-update-slice_fusion.2
  38.0 0.0 copy-done
  38.0 0.1 constant_dynamic-update-slice_fusion.1
  38.1 0.1 constant_dynamic-update-slice_fusion
  38.2 1.1 %constant_dynamic-slice_fusion = bf16[640,1536]{1,0:T(8,128)(2,1)S(1)} fusion(bf16[640,3072]{1,0:T(8,128)(2,1)S(1)} %constant_dynamic-update-slice_fusion, s32[]{:T(128)S(6)} %select_n.14), kind=kLoop, calls=%fused_computation.14 | loop fusion | bytes 3932164 | tf_op jit(solution)/shard_map/jit(_roll_dynamic)/dynamic_slice | solution.py:37
  39.4 4.0 %collective-permute-start.3 = (bf16[640,1536]{1,0:T(8,128)(2,1)S(1)}, bf16[640,1536]{1,0:T(8,128)(2,1)S(1)}, u32[]{:S(2)}, u32[]{:S(2)}) collective-permute-start(bf16[640,1536]{1,0:T(8,128)(2,1)S(1)} %constant_dynamic-slice_fusion), channel_id=1, source_target_pairs={{4,0},{8,4},{12,8},{5,1},{9,5},{13,9},{6,2},{10,6},{14,10},{7,3},{... | collective-permute-start | bytes 5898248 | tf_op jit(solution)/shard_map/ppermute | solution.py:10
  43.4 1.3 %fusion.2 = f32[384]{0:T(512)S(1)} fusion(bf16[640,1536]{1,0:T(8,128)(2,1)S(1)} %constant_dynamic-slice_fusion, bf16[640,384]{1,0:T(8,128)(2,1)S(1)} %copy-done), kind=kOutput, calls=%fused_computation.4 | convolution fusion | flops 756743808 | bytes 2459136 | tf_op jit(solution)/shard_map/dot_general | solution.py:18
  44.8 21.9 %collective-permute-done.3 = bf16[640,1536]{1,0:T(8,128)(2,1)S(1)} collective-permute-done((bf16[640,1536]{1,0:T(8,128)(2,1)S(1)}, bf16[640,1536]{1,0:T(8,128)(2,1)S(1)}, u32[]{:S(2)}, u32[]{:S(2)}) %collective-permute-start.3) | collective-permute-done | bytes 1966112 | tf_op jit(solution)/shard_map/ppermute | solution.py:10
  66.7 1.3 %fusion.3 = f32[384]{0:T(512)S(1)} fusion(bf16[640,1536]{1,0:T(8,128)(2,1)S(1)} %collective-permute-done.3, bf16[640,384]{1,0:T(8,128)(2,1)S(1)} %copy-done), kind=kOutput, calls=%fused_computation.5 | convolution fusion | flops 756743808 | bytes 2459136 | tf_op jit(solution)/shard_map/dot_general | solution.py:18
  68.0 0.6 add.16
Async XLA Ops:
  0.0 38.0 %copy-start = (bf16[640,384]{1,0:T(8,128)(2,1)S(1)}, bf16[640,384]{1,0:T(8,128)(2,1)}, u32[]{:S(2)}) copy-start(bf16[640,384]{1,0:T(8,128)(2,1)} %param.1) | copy-start | bytes 1474564
  0.0 15.4 %collective-permute-start = (bf16[640,384]{1,0:T(8,128)(2,1)}, bf16[640,384]{1,0:T(8,128)(2,1)S(1)}, u32[]{:S(2)}, u32[]{:S(2)}) collective-permute-start(bf16[640,384]{1,0:T(8,128)(2,1)} %param.1), channel_id=1, source_target_pairs={{0,1},{1,2},{2,3},{3,0},{4,5},{5,6},{6,7},{7,4},{8,9},{9,10},{10,1... | collective-permute-start | bytes 1474568 | tf_op jit(solution)/shard_map/ppermute | solution.py:30
  15.4 13.4 %collective-permute-start.1 = (bf16[640,384]{1,0:T(8,128)(2,1)S(1)}, bf16[640,384]{1,0:T(8,128)(2,1)S(1)}, u32[]{:S(2)}, u32[]{:S(2)}) collective-permute-start(bf16[640,384]{1,0:T(8,128)(2,1)S(1)} %collective-permute-done), channel_id=1, source_target_pairs={{0,1},{1,2},{2,3},{3,0},{4,5},{5,6},{6,7},{7,4},{8,9},{9,10},{10,1... | collective-permute-start | bytes 1474568 | tf_op jit(solution)/shard_map/ppermute | solution.py:30
  15.4 22.2 %collective-permute-start.2 = (bf16[640,384]{1,0:T(8,128)(2,1)}, bf16[640,384]{1,0:T(8,128)(2,1)S(1)}, u32[]{:S(2)}, u32[]{:S(2)}) collective-permute-start(bf16[640,384]{1,0:T(8,128)(2,1)} %param.1), channel_id=1, source_target_pairs={{0,3},{1,0},{2,1},{3,2},{4,7},{5,4},{6,5},{7,6},{8,11},{9,8},{10,9... | collective-permute-start | bytes 1474568 | tf_op jit(solution)/shard_map/ppermute | solution.py:33
  39.4 27.3 %collective-permute-start.3 = (bf16[640,1536]{1,0:T(8,128)(2,1)S(1)}, bf16[640,1536]{1,0:T(8,128)(2,1)S(1)}, u32[]{:S(2)}, u32[]{:S(2)}) collective-permute-start(bf16[640,1536]{1,0:T(8,128)(2,1)S(1)} %constant_dynamic-slice_fusion), channel_id=1, source_target_pairs={{4,0},{8,4},{12,8},{5,1},{9,5},{13,9},{6,2},{10,6},{14,10},{7,3},{... | collective-permute-start | bytes 5898248 | tf_op jit(solution)/shard_map/ppermute | solution.py:10
